TPU v7x, 512 devices: a whole 4x8x8 slice. The times are simulated.
512 devices in a mesh: blk: 16 (over y_hi, z), bank: 32 (over y_lo, x, core).
Axes of the slice: x: 4, y: 8 (y_hi: 2, y_lo: 4; y = y_hi * 4 + y_lo), z: 8, core: 2. Of those that a mesh axis runs over, the one named last changes fastest.
Arguments:
- log_density: bfloat16 [2048, 32768], P(('blk', 'bank')), may hold values from -8 to 8
- assignment: int32 [2048], P(('blk', 'bank')), may hold values from 0 to 7, as said below
Outputs:
- centers: bfloat16 [8, 32768], P(None, 'bank')
- potentials: float32 [2048, 32768], P(('blk', 'bank'))
Inputs may be any that keep to these rules, and one draw needn't show every extreme that they name: Every barycenter index is the assignment of at least one member.
All inputs are finite; a program needn't handle non-finite values.
Results may differ from a plain program's by a relative error of at most 0.0051.
Values may be sent and summed in bfloat16 or wider, within the bound.
No kernel may reach another device: no remote copies, remote signals or barrier semaphores. Data moves between devices by JAX's collectives and lax.ppermute only.
A program may use at most 64 MiB of HBM per device.

v0:
```python
import jax
import jax.numpy as jnp
from jax import lax
from jax.sharding import PartitionSpec as P

G = 32
BARS = 8
ITERS = 2


def kernel_tables():
    grid_pos = jnp.arange(G, dtype=jnp.float32)
    offset = grid_pos[:, None] - grid_pos[None, :]
    kernel_line = jnp.exp(-0.5 * offset * offset)
    kernel_pair = (
        (kernel_line[:, None, :, None] * kernel_line[None, :, None, :])
        .reshape(G * G, G * G)
        .astype(jnp.bfloat16)
    )
    return (kernel_line, kernel_pair)


def log_convolve(field_log, kernel_line, kernel_pair):
    member_count = field_log.shape[0]
    raised = jnp.exp(field_log).astype(jnp.bfloat16).reshape(member_count * G, G * G)
    inner_sum = jnp.dot(raised, kernel_pair, preferred_element_type=jnp.float32).reshape(
        member_count, G, G * G
    )
    outer_sum = jnp.einsum("ij,mjc->mic", kernel_line, inner_sum, precision=lax.Precision.HIGHEST)
    return jnp.log(outer_sum).reshape(member_count, G * G * G)


def per_device(log_density, assignment):
    kernel_line, kernel_pair = kernel_tables()
    member_count = log_density.shape[0]
    cell_count = log_density.shape[1]
    row_count = cell_count // 128
    labels = jnp.arange(BARS, dtype=jnp.int32)
    onehot = (assignment[:, None] == labels[None, :]).astype(jnp.float32)
    counts = lax.psum(jnp.sum(onehot, axis=0), ("blk", "bank"))
    selector = onehot.astype(jnp.bfloat16)
    member_weights = jnp.transpose(onehot)
    potential = jnp.zeros((member_count, cell_count), jnp.float32)
    center_owned = jnp.zeros((row_count // lax.axis_size("bank"), BARS, 128), jnp.bfloat16)
    for iteration in range(ITERS):
        source = log_density.astype(jnp.float32) - log_convolve(potential, kernel_line, kernel_pair)
        smoothed = log_convolve(source, kernel_line, kernel_pair)
        blocks = smoothed.reshape(member_count, row_count, 128)
        reduced = lax.psum_scatter(
            jnp.einsum("km,mrl->rkl", member_weights, blocks, precision=lax.Precision.HIGHEST),
            "bank",
            scatter_dimension=0,
            tiled=True,
        )
        summed = lax.psum(reduced, "blk")
        center_slice = (summed / counts[None, :, None]).astype(jnp.bfloat16)
        center_all = lax.all_gather(center_slice, "bank", axis=0, tiled=True)
        center_owned = center_slice
        chosen = jnp.einsum("mk,rkl->mrl", selector, center_all, preferred_element_type=jnp.float32)
        potential = chosen.reshape(member_count, cell_count) - smoothed
    centers = jnp.transpose(center_owned, (1, 0, 2)).reshape(BARS, center_owned.shape[0] * 128)
    return (centers, potential)


def solution(mesh):
    placed = (P(("blk", "bank"), None), P(("blk", "bank")))
    return jax.shard_map(
        per_device,
        mesh=mesh,
        in_specs=placed,
        out_specs=(P(None, "bank"), P(("blk", "bank"), None)),
        check_vma=False,
    )
```

profile of v0, /device:TPU:1, one launch (start us, length us, event | category | flops | bytes accessed | tf_op | source)
XLA Modules:
  0.0 615.1 jit_solution(17114058292738188008)
XLA Ops:
  7.2 0.0 reduce-scatter.3.cloned.1.call-start
  7.2 5.3 multiply_convert_fusion
  12.5 11.3 %reshape.101 = bf16[1024,1024,1]{1,0,2:T(8,128)(2,1)S(1)} reshape(bf16[32,32,32,32]{3,2,1,0:T(8,128)(2,1)} %multiply_convert_fusion) | data formatting | bytes 4194304 | tf_op jit(solution)/shard_map/convert_element_type | solution.py:18
  23.8 0.0 copy-start
  23.8 0.4 fusion.17
  24.3 0.6 fusion.3
  24.9 0.3 copy.9
  25.2 0.0 copy-done
  25.2 0.2 fusion.5
  25.4 0.0 copy-start.1
  25.5 0.5 fusion.14
  25.9 0.6 fusion.2
  26.5 0.1 reshape_reshape.6
  26.6 0.0 copy-done.1
  26.6 2.0 convolution_bitcast_fusion.2
  28.6 0.0 reduce-scatter.3.cloned.1.call-update
  28.6 0.0 reduce-scatter.5.cloned.1.call-start
  28.7 0.1 convert_reduce_fusion
  28.8 108.1 %psum.22 = f32[8]{0:T(128)S(1)} all-reduce(f32[8]{0:T(128)S(1)} %convert_reduce_fusion), channel_id=1, replica_groups=mesh['blk'=16,'bank'=32] {'blk','bank'}, use_global_device_ids=true, to_apply=%region_3.0 | all-reduce | flops 8 | bytes 64 | tf_op jit(solution)/shard_map/psum | solution.py:40
  136.9 42.7 %reduce-scatter.3.cloned.1.call-done = f32[8,8,128]{2,1,0:T(8,128)} async-done(((f32[256,8,128]{2,1,0:T(8,128)}), f32[8,8,128]{2,1,0:T(8,128)}) %reduce-scatter.3.cloned.1.call-update) | async-done | bytes 32784 | tf_op jit(solution)/shard_map/reduce_scatter | solution.py:49
  179.6 85.1 %psum.21 = f32[8,8,128]{2,1,0:T(8,128)S(1)} all-reduce(f32[8,8,128]{2,1,0:T(8,128)} %reduce-scatter.3.cloned.1.call-done), channel_id=1, replica_groups=mesh['blk'=16,'bank'=32] {'blk'}, use_global_device_ids=true, to_apply=%region_1.0 | all-reduce | flops 8192 | bytes 65536 | tf_op jit(solution)/shard_map/psum | solution.py:55
  264.7 0.1 divide_convert_fusion.1
  264.7 55.8 %all_gather.6 = bf16[256,8,128]{2,1,0:T(8,128)(2,1)S(1)} all-gather(bf16[8,8,128]{2,1,0:T(8,128)(2,1)S(1)} %divide_convert_fusion.1), channel_id=1, replica_groups=mesh['blk'=16,'bank'=32] {'bank'}, dimensions={0}, use_global_device_ids=true | all-gather | bytes 540672 | tf_op jit(solution)/shard_map/all_gather | solution.py:57
  320.6 0.3 fusion.37
  320.9 0.8 copy.6
  321.7 1.1 reshape.96
  322.9 0.5 fusion.10
  323.3 0.6 fusion.1
  323.9 0.3 copy.11
  324.3 0.2 fusion.7
  324.5 0.5 fusion.11
  325.0 0.6 convolution_log_fusion
  325.6 0.1 reshape_reshape.7
  325.7 2.0 convolution_bitcast_fusion.1
  327.6 0.0 reduce-scatter.5.cloned.1.call-update
  327.6 0.3 copy.13
  328.0 137.6 %reduce-scatter.5.cloned.1.call-done = f32[8,8,128]{2,1,0:T(8,128)} async-done(((f32[256,8,128]{2,1,0:T(8,128)}), f32[8,8,128]{2,1,0:T(8,128)}) %reduce-scatter.5.cloned.1.call-update) | async-done | bytes 32784 | tf_op jit(solution)/shard_map/reduce_scatter | solution.py:49
  465.6 85.1 %psum.23 = f32[8,8,128]{2,1,0:T(8,128)S(1)} all-reduce(f32[8,8,128]{2,1,0:T(8,128)} %reduce-scatter.5.cloned.1.call-done), channel_id=1, replica_groups=mesh['blk'=16,'bank'=32] {'blk'}, use_global_device_ids=true, to_apply=%region_5.0 | all-reduce | flops 8192 | bytes 65536 | tf_op jit(solution)/shard_map/psum | solution.py:55
  550.7 0.1 divide_convert_fusion
  550.8 0.7 fusion.58
  551.5 55.6 %all_gather.7 = bf16[256,8,128]{2,1,0:T(8,128)(2,1)S(1)} all-gather(bf16[8,8,128]{2,1,0:T(8,128)(2,1)S(1)} %divide_convert_fusion), channel_id=1, replica_groups=mesh['blk'=16,'bank'=32] {'bank'}, dimensions={0}, use_global_device_ids=true | all-gather | bytes 540672 | tf_op jit(solution)/shard_map/all_gather | solution.py:57
  607.1 1.1 fusion
  (1 shorter events, 0.0 us)
Async XLA Ops:
  7.2 172.4 %reduce-scatter.3.cloned.1.call-start = ((), (), s32[]{:S(2)}) async-start(), calls=%async_computation.2 | async-start | bytes 1081344 | tf_op jit(solution)/shard_map/reduce_scatter | solution.py:49
  23.8 1.4 copy-start
  25.4 1.2 copy-start.1
  28.6 436.9 %reduce-scatter.5.cloned.1.call-start = ((), (), s32[]{:S(2)}) async-start(), calls=%async_computation.3 | async-start | bytes 1081344 | tf_op jit(solution)/shard_map/reduce_scatter | solution.py:49
Sparse Core Ops, SparseCore 0:
  28.7 150.7 reduce-scatter.2
  327.8 137.7 reduce-scatter.4
where the time goes:
time: 616 us; the launch traced here: 615 us
  blocking collectives  390 us (63%)
  waiting for transfers between devices  180 us (29%)
  local copies, waits for them, and re-layouts  14.5 us (2%)
  between operations  14.2 us (2%)
  matrix products  9.63 us (2%)
  other arithmetic  6.6 us (1%)
    reduce_scatter x2, waiting for transfers between devices, per_device(): lax.psum_scatter(jnp.einsum('km,mrl->rkl', member_weights, blocks, precis...  180 us
    psum x2, blocking collectives, per_device(): summed = lax.psum(reduced, 'blk')  170 us
    all_gather x2, blocking collectives, per_device(): center_all = lax.all_gather(center_slice, 'bank', axis=0, tiled=True)  111 us
    psum x1, blocking collectives, per_device(): counts = lax.psum(jnp.sum(onehot, axis=0), ('blk', 'bank'))  108 us
  transfers between devices with their start and end apart: 2, of which 2 were waited for; matrix products, arithmetic and copies ran while one was open for 0% of the time, Pallas kernels for 0%

commit v1 on v0

--- a/solution.py
+++ b/solution.py
@@ -54,7 +54,9 @@
         )
         summed = lax.psum(reduced, "blk")
         center_slice = (summed / counts[None, :, None]).astype(jnp.bfloat16)
-        center_all = lax.all_gather(center_slice, "bank", axis=0, tiled=True)
+        center_all = jnp.concatenate(
+            lax.all_to_all(jnp.stack([center_slice] * lax.axis_size("bank")), "bank", 0, 0), axis=0
+        )
         center_owned = center_slice
         chosen = jnp.einsum("mk,rkl->mrl", selector, center_all, preferred_element_type=jnp.float32)
         potential = chosen.reshape(member_count, cell_count) - smoothed

time: 616 us -> 578 us (0.938)
  blocking collectives: 390 us -> 278 us
  starting transfers between devices: 0.08 us -> 42 us
  waiting for transfers between devices: 180 us -> 211 us
    all_gather x2 -> x0, blocking collectives: 111 us -> none  [per_device(): center_all = lax.all_gather(center_slice, 'bank', axis=0, tiled=True)]
    all_to_all x0 -> x2, starting transfers between devices: none -> 41.8 us  [per_device(): lax.all_to_all(jnp.stack([center_slice] * lax.axis_size('bank')), 'bank',...]
    all_to_all x0 -> x2, waiting for transfers between devices: none -> 30.7 us  [per_device(): lax.all_to_all(jnp.stack([center_slice] * lax.axis_size('bank')), 'bank',...]
  transfers between devices with their start and end apart: 2 -> 4, of which waited for: 2 -> 4; matrix products, arithmetic and copies ran while one was open for 0% -> 0% of each run, Pallas kernels for 0% -> 0%
where the time goes in v1:
time: 578 us
  blocking collectives  278 us (48%)
  waiting for transfers between devices  211 us (37%)
  starting transfers between devices  42 us (7%)
  local copies, waits for them, and re-layouts  15.5 us (3%)
  between operations  14.2 us (2%)
  matrix products  10.7 us (2%)
  other arithmetic  6.59 us (1%)
    reduce_scatter x2, waiting for transfers between devices, per_device(): lax.psum_scatter(jnp.einsum('km,mrl->rkl', member_weights, blocks, precis...  180 us
    psum x2, blocking collectives, per_device(): summed = lax.psum(reduced, 'blk')  170 us
    psum x1, blocking collectives, per_device(): counts = lax.psum(jnp.sum(onehot, axis=0), ('blk', 'bank'))  108 us
    all_to_all x2, starting transfers between devices, per_device(): lax.all_to_all(jnp.stack([center_slice] * lax.axis_size('bank')), 'bank',...  41.8 us
    all_to_all x2, waiting for transfers between devices, per_device(): lax.all_to_all(jnp.stack([center_slice] * lax.axis_size('bank')), 'bank',...  30.7 us
  transfers between devices with their start and end apart: 4, of which 4 were waited for; matrix products, arithmetic and copies ran while one was open for 0% of the time, Pallas kernels for 0%

profile of v1, /device:TPU:1, one launch (start us, length us, event | category | flops | bytes accessed | tf_op | source)
XLA Modules:
  0.0 577.6 jit_solution(9502267768342563470)
XLA Ops:
  7.2 0.0 reduce-scatter.3.cloned.1.call-start
  7.2 5.3 multiply_convert_fusion
  12.5 11.3 %reshape.114 = bf16[1024,1024,1]{1,0,2:T(8,128)(2,1)S(1)} reshape(bf16[32,32,32,32]{3,2,1,0:T(8,128)(2,1)} %multiply_convert_fusion) | data formatting | bytes 4194304 | tf_op jit(solution)/shard_map/convert_element_type | solution.py:18
  23.8 0.0 copy-start
  23.8 0.4 fusion.19
  24.3 0.6 fusion.3
  24.9 0.3 copy.8
  25.2 0.0 copy-done
  25.2 0.2 fusion.5
  25.4 0.0 copy-start.1
  25.5 0.5 fusion.16
  25.9 0.6 convolution_log_fusion.2
  26.5 0.1 reshape_reshape.6
  26.6 0.0 copy-done.1
  26.6 2.0 convolution_bitcast_fusion.1
  28.6 0.0 reduce-scatter.3.cloned.1.call-update
  28.6 0.1 convert_reduce_fusion
  28.7 108.2 %psum.22 = f32[8]{0:T(128)S(1)} all-reduce(f32[8]{0:T(128)S(1)} %convert_reduce_fusion), channel_id=1, replica_groups=mesh['blk'=16,'bank'=32] {'blk','bank'}, use_global_device_ids=true, to_apply=%region_3.0 | all-reduce | flops 8 | bytes 64 | tf_op jit(solution)/shard_map/psum | solution.py:40
  136.9 42.6 %reduce-scatter.3.cloned.1.call-done = f32[8,8,128]{2,1,0:T(8,128)} async-done(((f32[256,8,128]{2,1,0:T(8,128)}), f32[8,8,128]{2,1,0:T(8,128)}) %reduce-scatter.3.cloned.1.call-update) | async-done | bytes 32784 | tf_op jit(solution)/shard_map/reduce_scatter | solution.py:49
  179.5 84.6 %psum.21 = f32[8,8,128]{2,1,0:T(8,128)S(1)} all-reduce(f32[8,8,128]{2,1,0:T(8,128)} %reduce-scatter.3.cloned.1.call-done), channel_id=1, replica_groups=mesh['blk'=16,'bank'=32] {'blk'}, use_global_device_ids=true, to_apply=%region_1.0 | all-reduce | flops 8192 | bytes 65536 | tf_op jit(solution)/shard_map/psum | solution.py:55
  264.1 0.1 divide_convert_fusion.1
  264.2 0.9 stack.4
  265.1 21.0 %all-to-all-start = ((bf16[32,8,8,128]{3,2,1,0:T(8,128)(2,1)}), bf16[32,8,8,128]{3,2,1,0:T(8,128)(2,1)S(1)}, u32[]{:S(2)}, u32[]{:S(2)}) async-start(bf16[32,8,8,128]{3,2,1,0:T(8,128)(2,1)} %stack.4), calls=%async_computation.1 | async-start | bytes 1048576 | tf_op jit(solution)/shard_map/all_to_all | solution.py:58
  286.1 0.2 reduce-scatter.5.cloned.1.call-start
  286.4 1.1 copy.10
  287.5 15.2 %all-to-all-done = bf16[32,8,8,128]{3,2,1,0:T(8,128)(2,1)S(1)} async-done(((bf16[32,8,8,128]{3,2,1,0:T(8,128)(2,1)}), bf16[32,8,8,128]{3,2,1,0:T(8,128)(2,1)S(1)}, u32[]{:S(2)}, u32[]{:S(2)}) %all-to-all-start) | async-done | bytes 524320 | tf_op jit(solution)/shard_map/all_to_all | solution.py:58
  302.7 1.4 fusion.1
  304.1 0.5 fusion.13
  304.6 0.6 fusion.2
  305.2 0.3 copy.12
  305.5 0.2 fusion.7
  305.7 0.5 fusion.10
  306.2 0.6 convolution_log_fusion
  306.8 0.1 reshape_reshape.7
  306.9 2.0 convolution_bitcast_fusion
  308.9 0.0 reduce-scatter.5.cloned.1.call-update
  308.9 137.4 %reduce-scatter.5.cloned.1.call-done = f32[8,8,128]{2,1,0:T(8,128)} async-done(((f32[256,8,128]{2,1,0:T(8,128)}), f32[8,8,128]{2,1,0:T(8,128)}) %reduce-scatter.5.cloned.1.call-update) | async-done | bytes 32784 | tf_op jit(solution)/shard_map/reduce_scatter | solution.py:49
  446.3 85.0 %psum.23 = f32[8,8,128]{2,1,0:T(8,128)S(1)} all-reduce(f32[8,8,128]{2,1,0:T(8,128)} %reduce-scatter.5.cloned.1.call-done), channel_id=1, replica_groups=mesh['blk'=16,'bank'=32] {'blk'}, use_global_device_ids=true, to_apply=%region_5.0 | all-reduce | flops 8192 | bytes 65536 | tf_op jit(solution)/shard_map/psum | solution.py:55
  531.3 0.1 divide_convert_fusion
  531.4 0.9 stack.5
  532.3 20.7 %all-to-all-start.1 = ((bf16[32,8,8,128]{3,2,1,0:T(8,128)(2,1)}), bf16[32,8,8,128]{3,2,1,0:T(8,128)(2,1)S(1)}, u32[]{:S(2)}, u32[]{:S(2)}) async-start(bf16[32,8,8,128]{3,2,1,0:T(8,128)(2,1)} %stack.5), calls=%async_computation.3 | async-start | bytes 1048576 | tf_op jit(solution)/shard_map/all_to_all | solution.py:58
  553.0 0.3 copy.14
  553.4 0.7 fusion.56
  554.1 15.5 %all-to-all-done.1 = bf16[32,8,8,128]{3,2,1,0:T(8,128)(2,1)S(1)} async-done(((bf16[32,8,8,128]{3,2,1,0:T(8,128)(2,1)}), bf16[32,8,8,128]{3,2,1,0:T(8,128)(2,1)S(1)}, u32[]{:S(2)}, u32[]{:S(2)}) %all-to-all-start.1) | async-done | bytes 524320 | tf_op jit(solution)/shard_map/all_to_all | solution.py:58
  569.6 1.1 convolution_subtract_fusion
  (1 shorter events, 0.0 us)
Async XLA Ops:
  7.2 172.3 %reduce-scatter.3.cloned.1.call-start = ((), (), s32[]{:S(2)}) async-start(), calls=%async_computation.4 | async-start | bytes 1081344 | tf_op jit(solution)/shard_map/reduce_scatter | solution.py:49
  23.8 1.4 copy-start
  25.4 1.2 copy-start.1
  265.1 37.6 %all-to-all-start = ((bf16[32,8,8,128]{3,2,1,0:T(8,128)(2,1)}), bf16[32,8,8,128]{3,2,1,0:T(8,128)(2,1)S(1)}, u32[]{:S(2)}, u32[]{:S(2)}) async-start(bf16[32,8,8,128]{3,2,1,0:T(8,128)(2,1)} %stack.4), calls=%async_computation.1 | async-start | bytes 1048576 | tf_op jit(solution)/shard_map/all_to_all | solution.py:58
  286.1 160.2 %reduce-scatter.5.cloned.1.call-start = ((), (), s32[]{:S(2)}) async-start(), calls=%async_computation.5 | async-start | bytes 1081344 | tf_op jit(solution)/shard_map/reduce_scatter | solution.py:49
  532.3 37.3 %all-to-all-start.1 = ((bf16[32,8,8,128]{3,2,1,0:T(8,128)(2,1)}), bf16[32,8,8,128]{3,2,1,0:T(8,128)(2,1)S(1)}, u32[]{:S(2)}, u32[]{:S(2)}) async-start(bf16[32,8,8,128]{3,2,1,0:T(8,128)(2,1)} %stack.5), calls=%async_computation.3 | async-start | bytes 1048576 | tf_op jit(solution)/shard_map/all_to_all | solution.py:58
Sparse Core Ops, SparseCore 0:
  28.7 150.6 reduce-scatter.2
  309.0 137.2 reduce-scatter.4

commit v2 on v0

--- a/solution.py
+++ b/solution.py
@@ -52,7 +52,7 @@
             scatter_dimension=0,
             tiled=True,
         )
-        summed = lax.psum(reduced, "blk")
+        summed = jnp.sum(lax.all_gather(reduced, "blk"), axis=0)
         center_slice = (summed / counts[None, :, None]).astype(jnp.bfloat16)
         center_all = lax.all_gather(center_slice, "bank", axis=0, tiled=True)
         center_owned = center_slice

time: 616 us -> 531 us (0.86)
  blocking collectives: 390 us -> 304 us
    psum x2 -> x0, blocking collectives: 170 us -> none  [per_device(): summed = lax.psum(reduced, 'blk')]
    all_gather x0 -> x2, blocking collectives: none -> 97.8 us  [per_device(): summed = jnp.sum(lax.all_gather(reduced, 'blk'), axis=0)]
    all_gather x2, blocking collectives: 111 us -> 97.8 us  [per_device(): center_all = lax.all_gather(center_slice, 'bank', axis=0, tiled=True)]
where the time goes in v2:
time: 531 us; the launch traced here: 530 us
  blocking collectives  304 us (57%)
  waiting for transfers between devices  182 us (34%)
  local copies, waits for them, and re-layouts  14.5 us (3%)
  between operations  14.2 us (3%)
  matrix products  9.63 us (2%)
  other arithmetic  6.67 us (1%)
    reduce_scatter x2, waiting for transfers between devices, per_device(): lax.psum_scatter(jnp.einsum('km,mrl->rkl', member_weights, blocks, precis...  182 us
    psum x1, blocking collectives, per_device(): counts = lax.psum(jnp.sum(onehot, axis=0), ('blk', 'bank'))  108 us
    all_gather x2, blocking collectives, per_device(): center_all = lax.all_gather(center_slice, 'bank', axis=0, tiled=True)  97.8 us
    all_gather x2, blocking collectives, per_device(): summed = jnp.sum(lax.all_gather(reduced, 'blk'), axis=0)  97.8 us
    convert_element_type x1, local copies, waits for them, and re-layouts, kernel_tables(): kernel_pair = (kernel_line[:, None, :, None] * kernel_line[None, :, None,...  11.3 us
  transfers between devices with their start and end apart: 2, of which 2 were waited for; matrix products, arithmetic and copies ran while one was open for 0% of the time, Pallas kernels for 0%

profile of v2, /device:TPU:1, one launch (start us, length us, event | category | flops | bytes accessed | tf_op | source)
XLA Modules:
  0.0 530.5 jit_solution(10032098381937809484)
XLA Ops:
  7.2 0.0 reduce-scatter.3.cloned.1.call-start
  7.2 5.3 multiply_convert_fusion
  12.5 11.3 %reshape.103 = bf16[1024,1024,1]{1,0,2:T(8,128)(2,1)S(1)} reshape(bf16[32,32,32,32]{3,2,1,0:T(8,128)(2,1)} %multiply_convert_fusion) | data formatting | bytes 4194304 | tf_op jit(solution)/shard_map/convert_element_type | solution.py:18
  23.8 0.0 copy-start
  23.8 0.4 fusion.17
  24.3 0.6 fusion.3
  24.9 0.3 copy.10
  25.2 0.0 copy-done
  25.2 0.2 fusion.5
  25.4 0.0 copy-start.1
  25.5 0.5 fusion.14
  25.9 0.6 fusion.2
  26.5 0.1 reshape_reshape.6
  26.6 0.0 copy-done.1
  26.6 2.0 convolution_bitcast_fusion.2
  28.6 0.0 reduce-scatter.3.cloned.1.call-update
  28.6 0.0 reduce-scatter.5.cloned.1.call-start
  28.7 0.1 convert_reduce_fusion
  28.8 108.1 %psum.7 = f32[8]{0:T(128)S(1)} all-reduce(f32[8]{0:T(128)S(1)} %convert_reduce_fusion), channel_id=1, replica_groups=mesh['blk'=16,'bank'=32] {'blk','bank'}, use_global_device_ids=true, to_apply=%region_3.0 | all-reduce | flops 8 | bytes 64 | tf_op jit(solution)/shard_map/psum | solution.py:40
  136.9 43.4 %reduce-scatter.3.cloned.1.call-done = f32[8,8,128]{2,1,0:T(8,128)} async-done(((f32[256,8,128]{2,1,0:T(8,128)}), f32[8,8,128]{2,1,0:T(8,128)}) %reduce-scatter.3.cloned.1.call-update) | async-done | bytes 32784 | tf_op jit(solution)/shard_map/reduce_scatter | solution.py:49
  180.3 48.8 %all-gather = f32[128,8,128]{2,1,0:T(8,128)S(1)} all-gather(f32[8,8,128]{2,1,0:T(8,128)} %reduce-scatter.3.cloned.1.call-done), channel_id=2, replica_groups=mesh['blk'=16,'bank'=32] {'blk'}, dimensions={0}, use_global_device_ids=true | all-gather | bytes 557056 | tf_op jit(solution)/shard_map/all_gather | solution.py:55
  229.1 0.1 divide_convert_fusion.1
  229.2 49.1 %all_gather.20 = bf16[256,8,128]{2,1,0:T(8,128)(2,1)S(1)} all-gather(bf16[8,8,128]{2,1,0:T(8,128)(2,1)S(1)} %divide_convert_fusion.1), channel_id=1, replica_groups=mesh['blk'=16,'bank'=32] {'bank'}, dimensions={0}, use_global_device_ids=true | all-gather | bytes 540672 | tf_op jit(solution)/shard_map/all_gather | solution.py:57
  278.3 0.3 fusion.37
  278.7 0.8 copy.8
  279.5 1.1 reshape.96
  280.6 0.5 fusion.10
  281.1 0.6 fusion.1
  281.7 0.3 copy.12
  282.1 0.2 fusion.7
  282.3 0.5 fusion.11
  282.8 0.6 convolution_log_fusion
  283.4 0.1 reshape_reshape.7
  283.4 2.0 convolution_bitcast_fusion.1
  285.4 0.0 reduce-scatter.5.cloned.1.call-update
  285.4 0.3 copy.14
  285.8 138.2 %reduce-scatter.5.cloned.1.call-done = f32[8,8,128]{2,1,0:T(8,128)} async-done(((f32[256,8,128]{2,1,0:T(8,128)}), f32[8,8,128]{2,1,0:T(8,128)}) %reduce-scatter.5.cloned.1.call-update) | async-done | bytes 32784 | tf_op jit(solution)/shard_map/reduce_scatter | solution.py:49
  423.9 49.0 %all-gather.1 = f32[128,8,128]{2,1,0:T(8,128)S(1)} all-gather(f32[8,8,128]{2,1,0:T(8,128)} %reduce-scatter.5.cloned.1.call-done), channel_id=3, replica_groups=mesh['blk'=16,'bank'=32] {'blk'}, dimensions={0}, use_global_device_ids=true | all-gather | bytes 557056 | tf_op jit(solution)/shard_map/all_gather | solution.py:55
  473.0 0.1 divide_convert_fusion
  473.1 0.7 fusion.58
  473.8 48.7 %all_gather.23 = bf16[256,8,128]{2,1,0:T(8,128)(2,1)S(1)} all-gather(bf16[8,8,128]{2,1,0:T(8,128)(2,1)S(1)} %divide_convert_fusion), channel_id=1, replica_groups=mesh['blk'=16,'bank'=32] {'bank'}, dimensions={0}, use_global_device_ids=true | all-gather | bytes 540672 | tf_op jit(solution)/shard_map/all_gather | solution.py:57
  522.5 1.1 fusion
  (3 shorter events, 0.1 us)
Async XLA Ops:
  7.2 173.1 %reduce-scatter.3.cloned.1.call-start = ((), (), s32[]{:S(2)}) async-start(), calls=%async_computation.2 | async-start | bytes 1081344 | tf_op jit(solution)/shard_map/reduce_scatter | solution.py:49
  23.8 1.4 copy-start
  25.4 1.2 copy-start.1
  28.6 395.3 %reduce-scatter.5.cloned.1.call-start = ((), (), s32[]{:S(2)}) async-start(), calls=%async_computation.3 | async-start | bytes 1081344 | tf_op jit(solution)/shard_map/reduce_scatter | solution.py:49
Sparse Core Ops, SparseCore 0:
  28.7 151.4 reduce-scatter.2
  285.5 138.3 reduce-scatter.4
